TPU v7x, 128 devices: a whole 4x4x4 slice. The times are simulated.
128 devices in a mesh: req: 32 (over z, y, core), seq: 4 (over x).
Axes of the slice: x: 4, y: 4, z: 4, core: 2. Of those that a mesh axis runs over, the one named last changes fastest.
Arguments:
- hidden: bfloat16 [32, 4, 512, 2048], P('req', 'seq'), may hold values from -6 to 6
- w_in: bfloat16 [2048, 4384], P('req', 'seq'), may hold values from -0.125 to 0.125
- conv_weight: float32 [4, 2304], replicated, may hold values from -3 to 3
- conv_bias: float32 [2304], replicated, may hold values from -0.5 to 0.5
- dt_bias: float32 [32], replicated, may hold values from -5 to -2
- a_log: float32 [32], replicated, may hold values from -12 to 2
- d_skip: float32 [32], replicated, may hold values from 0.5 to 1.5
- norm_weight: float32 [2048], replicated, may hold values from 0.5 to 1.5
- lengths: int32 [32], replicated, may hold values from 4 to 512, as said below
- prompt_group: int32 [32], replicated, may hold values from 0 to 31, each once
Outputs:
- gated_out: bfloat16 [32, 4, 512, 2048], P('req', 'seq')
- final_states: float32 [32, 32, 64, 128], P(None, 'req', 'seq')
Inputs may be any that keep to these rules, and one draw needn't show every extreme that they name: Every prompt has 4 * lengths[p] tokens; some prompt has exactly 512 a device. Group prompt_group[p] holds prompt p; each group holds one prompt.
All inputs are finite; a program needn't handle non-finite values.
Results may differ from a plain program's by a relative error of at most 0.0059.
Values may be sent and summed in bfloat16 or wider, within the bound.
No kernel may reach another device: no remote copies, remote signals or barrier semaphores. Data moves between devices by JAX's collectives and lax.ppermute only.
A program may use at most 128 MiB of HBM per device.

v0:
```python
import jax
import jax.numpy as jnp
from jax import lax
from jax.sharding import PartitionSpec as P

BLOCK = 256


def shifted(block, axis, distance):
    devices = range(lax.axis_size(axis))
    route = [(i - distance, i) for i in devices if i - distance in devices]
    return lax.ppermute(block, axis, route)


def block_step(state, pieces):
    inputs_x, b_rows, c_rows, step_dt, log_decay = pieces
    length = inputs_x.shape[0]
    heads = step_dt.shape[1]
    hdim = inputs_x.shape[1] // heads
    running = jnp.cumsum(log_decay, axis=0)
    gram = jnp.einsum("tn,un->tu", c_rows, b_rows, preferred_element_type=jnp.float32)
    later = jnp.arange(length)[:, None] >= jnp.arange(length)[None, :]
    spread = running.T[:, :, None] - running.T[:, None, :]
    decay = jnp.where(later[None], jnp.exp(jnp.where(later[None], spread, 0.0)), 0.0)
    mixing = (gram[None] * decay * step_dt.T[:, None, :]).astype(jnp.bfloat16)
    heads_x = inputs_x.reshape(length, heads, hdim)
    inside = jnp.einsum("htu,uhp->thp", mixing, heads_x, preferred_element_type=jnp.float32)
    carried = jnp.exp(running)[:, :, None] * jnp.einsum(
        "tn,hpn->thp", c_rows.astype(jnp.float32), state, precision=lax.Precision.HIGHEST
    )
    final_log = running[-1]
    weighting = jnp.exp(final_log[None, :] - running) * step_dt
    weighted = (
        (heads_x.astype(jnp.float32) * weighting[:, :, None])
        .astype(jnp.bfloat16)
        .reshape(length, heads * hdim)
    )
    contrib = jnp.einsum("ud,un->dn", weighted, b_rows, preferred_element_type=jnp.float32).reshape(
        heads, hdim, -1
    )
    new_state = jnp.exp(final_log)[:, None, None] * state + contrib
    return (new_state, (inside + carried).reshape(length, heads * hdim))


def local(
    hidden, w_in, conv_weight, conv_bias, dt_bias, a_log, d_skip, norm_weight, lengths, prompt_group
):
    tok_rows = hidden[0, 0]
    slots = tok_rows.shape[0]
    inner = norm_weight.shape[0]
    heads = dt_bias.shape[0]
    hdim = inner // heads
    nstate = (conv_bias.shape[0] - inner) // 2
    convdim = conv_bias.shape[0]
    taps = conv_weight.shape[0]
    seq_count = lax.axis_size("seq")
    my_group = lax.axis_index("req")
    my_block = lax.axis_index("seq")
    qlen = jnp.sum(jnp.where(prompt_group == my_group, lengths, 0))
    filled = jnp.arange(slots, dtype=jnp.int32) < qlen
    wide_rows = lax.all_gather(w_in, "seq", axis=1, tiled=True)
    projected = jnp.dot(
        tok_rows,
        lax.all_gather(wide_rows, "req", axis=0, tiled=True),
        preferred_element_type=jnp.float32,
    ).astype(jnp.bfloat16)
    gate_z = projected[:, :inner]
    conv_in = projected[:, inner : inner + convdim]
    dt_raw = projected[:, inner + convdim :]
    edge_rows = lax.dynamic_slice_in_dim(conv_in, qlen - (taps - 1), taps - 1, 0)
    prev_edge = shifted(edge_rows, "seq", 1)
    extended = jnp.concatenate([prev_edge, conv_in], axis=0)
    accum = jnp.zeros((slots, convdim), jnp.float32) + conv_bias[None, :]
    for tap_index in range(taps):
        accum = accum + conv_weight[tap_index][None, :] * extended[
            tap_index : tap_index + slots
        ].astype(jnp.float32)
    conv_act = jax.nn.silu(accum).astype(jnp.bfloat16)
    inputs_x = conv_act[:, :inner]
    b_rows = conv_act[:, inner : inner + nstate]
    c_rows = conv_act[:, inner + nstate :]
    step_dt = jnp.where(
        filled[:, None], jax.nn.softplus(dt_raw.astype(jnp.float32) + dt_bias[None, :]), 0.0
    )
    log_decay = step_dt * (-jnp.exp(a_log))[None, :]
    through = jnp.cumsum(log_decay, axis=0)
    block_total = through[-1]
    block_rows = min(BLOCK, slots)
    count = slots // block_rows
    pieces = (
        inputs_x.reshape(count, block_rows, inner),
        b_rows.reshape(count, block_rows, nstate),
        c_rows.reshape(count, block_rows, nstate),
        step_dt.reshape(count, block_rows, heads),
        log_decay.reshape(count, block_rows, heads),
    )
    zero_state = jnp.zeros((heads, hdim, nstate), jnp.float32)
    local_end = zero_state
    outs = []
    for index in range(count):
        local_end, out = block_step(local_end, tuple((piece[index] for piece in pieces)))
        outs.append(out)
    outputs = jnp.concatenate(outs, axis=0)
    total_hi = lax.reduce_precision(block_total, exponent_bits=8, mantissa_bits=7)
    total_rest = block_total - total_hi
    total_mid = lax.reduce_precision(total_rest, exponent_bits=8, mantissa_bits=7)
    total_lo = total_rest - total_mid
    parts = jnp.stack([total_hi, total_mid, total_lo], axis=1).astype(jnp.bfloat16)
    parts = jnp.broadcast_to(parts[:, :, None], (heads, 3, 128))
    packed = jnp.concatenate(
        [
            local_end.reshape(heads, hdim * nstate).astype(jnp.bfloat16),
            parts.reshape(heads, 3 * 128),
        ],
        axis=1,
    )
    gathered = lax.all_gather(packed, "seq", axis=0, tiled=False)
    ends = (
        gathered[:, :, : hdim * nstate].astype(jnp.float32).reshape(seq_count, heads, hdim, nstate)
    )
    sent = gathered[:, :, hdim * nstate :].astype(jnp.float32)
    totals = sent[:, :, 0] + (sent[:, :, 128] + sent[:, :, 256])
    entering = zero_state
    for turn in range(seq_count - 1):
        stepped = jnp.exp(totals[turn])[:, None, None] * entering + ends[turn]
        entering = jnp.where(turn < my_block, stepped, entering)
    incoming = jnp.exp(through)[:, :, None] * jnp.einsum(
        "tn,hpn->thp", c_rows.astype(jnp.float32), entering, precision=lax.Precision.HIGHEST
    )
    heads_y = (
        outputs.reshape(slots, heads, hdim)
        + incoming
        + d_skip[None, :, None] * inputs_x.astype(jnp.float32).reshape(slots, heads, hdim)
    )
    gated = heads_y.reshape(slots, inner) * jax.nn.silu(gate_z.astype(jnp.float32))
    scale = lax.rsqrt(jnp.mean(gated * gated, axis=1, keepdims=True) + 1e-05)
    normed = jnp.where(filled[:, None], gated * scale * norm_weight[None, :], 0.0)
    gated_out = normed.astype(jnp.bfloat16).reshape(1, 1, slots, inner)
    later_mask = jnp.arange(seq_count)[None, :] > jnp.arange(seq_count)[:, None]
    after = jnp.sum(jnp.where(later_mask[:, :, None], totals[None, :, :], 0.0), axis=1)
    piece = hdim // seq_count
    own_ends = lax.dynamic_slice_in_dim(ends, my_block * piece, piece, axis=2)
    share = jnp.sum(jnp.exp(after)[:, :, None, None] * own_ends, axis=0)
    moved = lax.all_to_all(share[None], "req", split_axis=1, concat_axis=0, tiled=True)
    final_states = jnp.take(moved, prompt_group, axis=0)
    return (gated_out, final_states)


def solution(mesh):
    in_specs = (
        P("req", "seq", None, None),
        P("req", "seq"),
        P(),
        P(),
        P(),
        P(),
        P(),
        P(),
        P(),
        P(),
    )
    out_specs = (P("req", "seq", None, None), P(None, "req", "seq", None))
    return jax.shard_map(local, mesh=mesh, in_specs=in_specs, out_specs=out_specs, check_vma=False)
```

profile of v0, /device:TPU:1, one launch (start us, length us, event | category | flops | bytes accessed | tf_op | source)
XLA Modules:
  0.0 217.0 jit_solution(9497161019344867276)
XLA Ops:
  7.2 12.8 %all-gather.1 = bf16[4,1096,64]{1,2,0:T(8,128)(2,1)S(1)} all-gather(bf16[1,1096,64]{1,2,0:T(8,128)(2,1)} %bitcast.194), channel_id=1, replica_groups=mesh['req'=32,'seq'=4] {'seq'}, dimensions={0}, use_global_device_ids=true | all-gather | bytes 701440 | tf_op jit(solution)/shard_map/all_gather | solution.py:61
  20.1 0.5 copy.74
  20.5 1.2 reshape.358
  21.8 1.3 compare_select_fusion.1
  24.5 0.7 iota_compare_fusion.2
  25.1 1.0 slice_reduce_fusion.9
  26.2 0.7 compare_and_fusion
  26.8 0.7 exponential_negate_fusion
  27.5 75.2 %all-gather.5.cloned.1.call-done = bf16[2048,4384]{1,0:T(8,128)(2,1)} async-done(((bf16[64,4384]{1,0:T(8,128)(2,1)}), bf16[2048,4384]{1,0:T(8,128)(2,1)}) %all-gather.5.cloned.1.call-update) | async-done | bytes 17956880 | tf_op jit(solution)/shard_map/all_gather | solution.py:64
  102.7 15.3 %convolution_convert_fusion = bf16[512,4384]{0,1:T(8,128)(2,1)} fusion(bf16[2048,4384]{1,0:T(8,128)(2,1)} %all-gather.5.cloned.1.call-done, bf16[1,1,512,2048]{3,2,1,0:T(8,128)(2,1)S(1)} %copy-done), kind=kOutput, calls=%fused_computation.3 | convolution fusion | flops 9196158976 | bytes 24543232 | tf_op jit(solution)/shard_map/dot_general | solution.py:62
  118.0 1.8 slice.193
  119.9 0.9 fusion.62
  120.8 0.6 reduce-window.20
  121.6 0.7 copy_bitcast_fusion.3
  122.5 0.6 reduce-window.24
  123.3 0.7 fusion.61
  124.7 3.3 %collective-permute-start = (bf16[3,2304]{1,0:T(4,128)(2,1)S(1)}, bf16[3,2304]{1,0:T(4,128)(2,1)S(1)}, u32[]{:S(2)}, u32[]{:S(2)}) collective-permute-start(bf16[3,2304]{1,0:T(4,128)(2,1)S(1)} %copy.75), channel_id=1, source_target_pairs={{0,1},{1,2},{2,3},{4,5},{5,6},{6,7},{8,9},{9,10},{10,11},{12,13},{... | collective-permute-start | bytes 41480 | tf_op jit(solution)/shard_map/ppermute | solution.py:12
  128.0 0.5 exponential_multiply_fusion.2
  128.5 1.2 reduce-window.26
  130.1 0.7 exponential_multiply_fusion
  130.9 0.5 exp.98
  132.0 10.5 %multiply_convert_fusion.2 = bf16[512,2304]{0,1:T(8,128)(2,1)S(1)} fusion(bf16[512,2304]{0,1:T(8,128)(2,1)} %copy-done.2, bf16[3,2304]{0,1:T(8,128)(2,1)S(1)} %copy.76, f32[2304]{0:T(1024)S(1)} %get-tuple-element.17, f32[2304]{0:T(1024)S(1)} %get-tuple-element.18, f32[2304]{0:T(1024)S(1)} %get-tuple-element.16, f32[2304]{0:T(1024)S(1)} %get-tuple-element.15, ...), kind=kLoop, calls=%fused_computation.6 | loop fusion | flops 30670848 | bytes 4778496 | tf_op jit(solution)/shard_map/convert_element_type | solution.py:78
  142.5 0.4 fusion.22
  143.4 0.5 fusion.25
  144.2 0.9 pad_maximum_fusion.1
  145.1 0.5 iota_compare_fusion.1
  145.7 1.4 slice.227
  147.5 1.0 fusion.29
  148.5 1.0 fusion.37
  149.7 4.4 %bitcast_add_fusion.1 = f32[256,32,64]{0,2,1:T(8,128)} fusion(f32[256,32,64]{0,2,1:T(8,128)S(1)} %fusion.29, bf16[256,32,64]{0,2,1:T(8,128)(2,1)S(1)} %bitcast.192, f32[32,256]{1,0:T(8,128)S(1)} %copy-done.8, f32[32,256]{1,0:T(8,128)S(1)} %copy-done.4, f32[256,256]{1,0:T(8,128)S(1)} %fusion.46, pred[256,256]{1,0:T(8,128)(4,1)S(1)} %iota_compare_fusion, ...), kind=kOutput, calls=%fused_computation.44 | convolution fusion | flops 282066944 | bytes 5668864 | tf_op jit(solution)/shard_map/htu,uhp->thp/dot_general | solution.py:27
  154.2 4.3 %bitcast_add_fusion = f32[256,32,64]{0,2,1:T(8,128)} fusion(f32[256,32,64]{0,2,1:T(8,128)S(1)} %fusion.37, bf16[256,32,64]{0,2,1:T(8,128)(2,1)S(1)} %bitcast.191, f32[32,256]{1,0:T(8,128)S(1)} %copy-done.6, f32[32,256]{1,0:T(8,128)S(1)} %copy-done.5, f32[256,256]{1,0:T(8,128)S(1)} %fusion.41, pred[256,256]{1,0:T(8,128)(4,1)S(1)} %iota_compare_fusion, ...), kind=kOutput, calls=%fused_computation.43 | convolution fusion | flops 282066944 | bytes 5668864 | tf_op jit(solution)/shard_map/htu,uhp->thp/dot_general | solution.py:27
  158.5 17.3 %all-gather.7.cloned.1.call-done = bf16[128,8576]{1,0:T(8,128)(2,1)} async-done(((bf16[32,8576]{1,0:T(8,128)(2,1)}), bf16[128,8576]{1,0:T(8,128)(2,1)}) %all-gather.7.cloned.1.call-update) | async-done | bytes 2195472 | tf_op jit(solution)/shard_map/all_gather | solution.py:117
  175.8 2.0 slice_convert_fusion
  177.8 0.9 slice_convert_fusion.1
  178.7 1.6 slice_bitcast_fusion.2
  180.2 0.7 copy.112
  181.2 0.9 multiply_reduce_fusion.1
  182.1 7.8 %all-to-all-start = ((f32[1,32,16,128]{3,2,0,1:T(8,128)}), f32[1,32,16,128]{3,2,0,1:T(8,128)}, u32[]{:S(2)}, u32[]{:S(2)}) async-start(f32[1,32,16,128]{3,2,0,1:T(8,128)} %bitcast.190), calls=%async_computation | async-start | bytes 524288 | tf_op jit(solution)/shard_map/all_to_all | solution.py:144
  189.9 1.4 copy.109
  191.3 1.4 copy.110
  193.1 0.8 fusion.26
  193.9 1.9 fusion.32
  195.8 3.7 %fusion.6 = f32[512,32,64]{0,2,1:T(8,128)S(1)} fusion(f32[256,32,64]{0,2,1:T(8,128)} %bitcast_add_fusion, f32[256,32,64]{0,2,1:T(8,128)} %bitcast_add_fusion.1, bf16[512,32,64]{0,2,1:T(8,128)(2,1)S(1)} %bitcast.181, f32[512,32,64]{0,2,1:T(8,128)S(1)} %fusion.32, f32[32]{0:T(128)S(1)} %copy-done.13, f32[512,32]{0,1:T(8,128)S(1)} %fusion.59), kind=kLoop, calls=%fused_computation.14 | loop fusion | flops 6291456 | bytes 14745728 | tf_op jit(solution)/shard_map/add | solution.py:131
  199.6 1.4 multiply_reduce_fusion
  201.0 2.9 %fusion.21 = bf16[1,1,512,2048]{2,3,1,0:T(8,128)(2,1)} fusion(f32[2048]{0:T(1024)S(1)} %copy-done.11, f32[512]{0:T(512)S(1)} %add_rsqrt_fusion, pred[512]{0:T(512)(128)(4,1)S(1)} %iota_compare_fusion.2, bf16[512,4384]{0,1:T(8,128)(2,1)S(1)} %bitcast.180, f32[512,32,64]{0,2,1:T(8,128)S(1)} %fusion.6), kind=kLoop, calls=%fused_computation.37 | loop fusion | flops 10485760 | bytes 8399360 | tf_op jit(solution)/shard_map/reshape | solution.py:138
  203.9 3.9 %copy.89 = bf16[1,1,512,2048]{3,2,1,0:T(8,128)(2,1)} copy(bf16[1,1,512,2048]{2,3,1,0:T(8,128)(2,1)} %fusion.21) | data formatting | bytes 4194304
  207.9 1.5 gather_fusion
  209.4 0.8 fusion.31
  (83 shorter events, 4.5 us)
Async XLA Ops:
  7.2 95.5 %copy-start = (bf16[1,1,512,2048]{3,2,1,0:T(8,128)(2,1)S(1)}, bf16[1,1,512,2048]{3,2,1,0:T(8,128)(2,1)}, u32[]{:S(2)}) copy-start(bf16[1,1,512,2048]{3,2,1,0:T(8,128)(2,1)} %param.10) | copy-start | bytes 6291460
  7.2 95.5 %all-gather.5.cloned.1.call-start = ((), (), s32[]{:S(2)}) async-start(), calls=%async_computation.1 | async-start | bytes 18923520 | tf_op jit(solution)/shard_map/all_gather | solution.py:64
  21.8 154.0 %all-gather.7.cloned.1.call-start = ((), (), s32[]{:S(2)}) async-start(), calls=%async_computation.2 | async-start | bytes 2744320 | tf_op jit(solution)/shard_map/all_gather | solution.py:117
  118.0 1.9 copy-start.12
  118.0 14.0 %copy-start.10 = (f32[2304]{0:T(1024)S(1)}, f32[2304]{0:T(1024)}, u32[]{:S(2)}) copy-start(f32[2304]{0:T(1024)} %param.13) | copy-start | bytes 27652
  119.9 12.1 %copy-start.2 = (bf16[512,2304]{0,1:T(8,128)(2,1)}, bf16[512,2304]{0,1:T(8,128)(2,1)S(1)}, u32[]{:S(2)}) copy-start(bf16[512,2304]{0,1:T(8,128)(2,1)S(1)} %slice.193) | copy-start | bytes 7077892
  124.7 6.9 %collective-permute-start = (bf16[3,2304]{1,0:T(4,128)(2,1)S(1)}, bf16[3,2304]{1,0:T(4,128)(2,1)S(1)}, u32[]{:S(2)}, u32[]{:S(2)}) collective-permute-start(bf16[3,2304]{1,0:T(4,128)(2,1)S(1)} %copy.75), channel_id=1, source_target_pairs={{0,1},{1,2},{2,3},{4,5},{5,6},{6,7},{8,9},{9,10},{10,11},{12,13},{... | collective-permute-start | bytes 41480 | tf_op jit(solution)/shard_map/ppermute | solution.py:12
  132.0 10.9 %copy-start.14 = (f32[32]{0:T(128)S(1)}, f32[32]{0:T(128)}, u32[]{:S(2)}) copy-start(f32[32]{0:T(128)} %exponential_multiply_fusion.2) | copy-start | bytes 388
  142.5 0.9 copy-start.15
  148.5 1.2 copy-start.4
  148.5 1.2 copy-start.8
  148.5 1.2 copy-start.9
  149.7 4.5 %copy-start.5 = (f32[32,256]{1,0:T(8,128)S(1)}, f32[32,256]{1,0:T(8,128)}, u32[]{:S(2)}) copy-start(f32[32,256]{1,0:T(8,128)} %get-tuple-element.40) | copy-start | bytes 98308
  149.7 4.4 %copy-start.6 = (f32[32,256]{1,0:T(8,128)S(1)}, f32[32,256]{1,0:T(8,128)}, u32[]{:S(2)}) copy-start(f32[32,256]{1,0:T(8,128)} %get-tuple-element.32) | copy-start | bytes 98308
  149.7 4.4 %copy-start.7 = (f32[256,32]{0,1:T(8,128)S(1)}, f32[256,32]{0,1:T(8,128)}, u32[]{:S(2)}) copy-start(f32[256,32]{0,1:T(8,128)} %get-tuple-element.38) | copy-start | bytes 98308
  180.2 0.8 copy-start.16
  182.1 25.7 %all-to-all-start = ((f32[1,32,16,128]{3,2,0,1:T(8,128)}), f32[1,32,16,128]{3,2,0,1:T(8,128)}, u32[]{:S(2)}, u32[]{:S(2)}) async-start(f32[1,32,16,128]{3,2,0,1:T(8,128)} %bitcast.190), calls=%async_computation | async-start | bytes 524288 | tf_op jit(solution)/shard_map/all_to_all | solution.py:144
  193.1 2.7 %copy-start.3 = (bf16[512,2048]{0,1:T(8,128)(2,1)S(1)}, bf16[512,2048]{0,1:T(8,128)(2,1)}, u32[]{:S(2)}) copy-start(bf16[512,2048]{0,1:T(8,128)(2,1)} %slice.227) | copy-start | bytes 6291460
  193.1 2.7 %copy-start.13 = (f32[32]{0:T(128)S(1)}, f32[32]{0:T(128)}, u32[]{:S(2)}) copy-start(f32[32]{0:T(128)} %param.16) | copy-start | bytes 388
  193.8 5.7 %slice-start = ((s8[4489216]{0:T(1024)(128)(4,1)}), s8[4194304]{0:T(1024)(128)(4,1)S(1)}, s32[]{:S(2)}) async-start(s8[4489216]{0:T(1024)(128)(4,1)} %bitcast.179), calls=%async_computation.3 | async-start | bytes 8388608
  195.8 3.8 %slice-start.1 = ((s8[4489216]{0:T(1024)(128)(4,1)}), s8[294912]{0:T(1024)(128)(4,1)S(1)}, s32[]{:S(2)}) async-start(s8[4489216]{0:T(1024)(128)(4,1)} %bitcast.179), calls=%async_computation.4 | async-start | bytes 589824
  199.6 1.4 copy-start.11
  201.0 9.2 %copy-start.1 = (bf16[1,1,512,2048]{3,2,1,0:T(8,128)(2,1)S(1)}, bf16[1,1,512,2048]{3,2,1,0:T(8,128)(2,1)}, u32[]{:S(2)}) copy-start(bf16[1,1,512,2048]{3,2,1,0:T(8,128)(2,1)} %param.10) | copy-start | bytes 6291460
Sparse Core Ops, SparseCore 0:
  21.9 80.7 all-gather.4
  145.2 30.5 all-gather.6
where the time goes:
time: 218 us; the launch traced here: 217 us
  waiting for transfers between devices  92.5 us (42%)
  other arithmetic  35.5 us (16%)
  matrix products  29.2 us (13%)
  local copies, waits for them, and re-layouts  20 us (9%)
  between operations  15.9 us (7%)
  blocking collectives  12.8 us (6%)
  starting transfers between devices  11.1 us (5%)
    all_gather x1, waiting for transfers between devices, local(): lax.all_gather(wide_rows, 'req', axis=0, tiled=True)  75.2 us
    all_gather x1, waiting for transfers between devices, local(): gathered = lax.all_gather(packed, 'seq', axis=0, tiled=False)  17.3 us
    dot_general x1, matrix products, local(): jnp.dot(tok_rows, lax.all_gather(wide_rows, 'req', axis=0, tiled=True), p...  15.3 us
    all_gather x1, blocking collectives, local(): wide_rows = lax.all_gather(w_in, 'seq', axis=1, tiled=True)  12.8 us
    unnamed x48, local copies, waits for them, and re-layouts  10.9 us
    convert_element_type x1, other arithmetic, local(): conv_act = jax.nn.silu(accum).astype(jnp.bfloat16)  10.5 us
    dot_general x2, matrix products, block_step(): jnp.einsum('htu,uhp->thp', mixing, heads_x, preferred_element_type=jnp.fl...  8.76 us
    all_to_all x1, starting transfers between devices, local(): lax.all_to_all(share[None], 'req', split_axis=1, concat_axis=0, tiled=True)  7.77 us
  transfers between devices with their start and end apart: 4, of which 2 were waited for; matrix products, arithmetic and copies ran while one was open for 18% of the time, Pallas kernels for 0%

commit v1 on v0

--- a/solution.py
+++ b/solution.py
@@ -141,7 +141,15 @@
     piece = hdim // seq_count
     own_ends = lax.dynamic_slice_in_dim(ends, my_block * piece, piece, axis=2)
     share = jnp.sum(jnp.exp(after)[:, :, None, None] * own_ends, axis=0)
-    moved = lax.all_to_all(share[None], "req", split_axis=1, concat_axis=0, tiled=True)
+    moved = jnp.concatenate(
+        lax.all_to_all(
+            jnp.stack(jnp.split(share[None], lax.psum(1, axis_name="req"), 1), 0),
+            axis_name="req",
+            split_axis=0,
+            concat_axis=0,
+        ),
+        0,
+    )
     final_states = jnp.take(moved, prompt_group, axis=0)
     return (gated_out, final_states)
 

time: 218 us -> 236 us (1.083)
  local copies, waits for them, and re-layouts: 20 us -> 39.1 us
    unnamed x48 -> x79, local copies, waits for them, and re-layouts: 10.9 us -> 29.5 us
  transfers between devices with their start and end apart: 4 -> 4, of which waited for: 2 -> 2; matrix products, arithmetic and copies ran while one was open for 18% -> 17% of each run, Pallas kernels for 0% -> 0%
where the time goes in v1:
time: 236 us
  waiting for transfers between devices  92.5 us (39%)
  local copies, waits for them, and re-layouts  39.1 us (17%)
  other arithmetic  34.8 us (15%)
  matrix products  29.2 us (12%)
  between operations  15.9 us (7%)
  blocking collectives  12.8 us (5%)
  starting transfers between devices  11.1 us (5%)
    all_gather x1, waiting for transfers between devices, local(): lax.all_gather(wide_rows, 'req', axis=0, tiled=True)  75.2 us
    unnamed x79, local copies, waits for them, and re-layouts  29.5 us
    all_gather x1, waiting for transfers between devices, local(): gathered = lax.all_gather(packed, 'seq', axis=0, tiled=False)  17.3 us
    dot_general x1, matrix products, local(): jnp.dot(tok_rows, lax.all_gather(wide_rows, 'req', axis=0, tiled=True), p...  15.3 us
    all_gather x1, blocking collectives, local(): wide_rows = lax.all_gather(w_in, 'seq', axis=1, tiled=True)  12.8 us
    convert_element_type x1, other arithmetic, local(): conv_act = jax.nn.silu(accum).astype(jnp.bfloat16)  10.5 us
    dot_general x2, matrix products, block_step(): jnp.einsum('htu,uhp->thp', mixing, heads_x, preferred_element_type=jnp.fl...  8.76 us
    all_to_all x1, starting transfers between devices, local(): lax.all_to_all(jnp.stack(jnp.split(share[None], lax.psum(1, axis_name='re...  7.77 us
  transfers between devices with their start and end apart: 4, of which 2 were waited for; matrix products, arithmetic and copies ran while one was open for 17% of the time, Pallas kernels for 0%

profile of v1, /device:TPU:1, one launch (start us, length us, event | category | flops | bytes accessed | tf_op | source)
XLA Modules:
  0.0 235.5 jit_solution(11292906508521311029)
XLA Ops:
  7.2 12.8 %all-gather.1 = bf16[4,1096,64]{1,2,0:T(8,128)(2,1)S(1)} all-gather(bf16[1,1096,64]{1,2,0:T(8,128)(2,1)} %bitcast.349), channel_id=1, replica_groups=mesh['req'=32,'seq'=4] {'seq'}, dimensions={0}, use_global_device_ids=true | all-gather | bytes 701440 | tf_op jit(solution)/shard_map/all_gather | solution.py:61
  20.5 1.2 reshape.359
  21.8 1.3 compare_select_fusion.1
  24.5 0.7 iota_compare_fusion.2
  25.1 1.0 slice_reduce_fusion.9
  26.2 0.7 compare_and_fusion
  26.8 0.7 exponential_negate_fusion
  27.5 75.2 %all-gather.5.cloned.1.call-done = bf16[2048,4384]{1,0:T(8,128)(2,1)} async-done(((bf16[64,4384]{1,0:T(8,128)(2,1)}), bf16[2048,4384]{1,0:T(8,128)(2,1)}) %all-gather.5.cloned.1.call-update) | async-done | bytes 17956880 | tf_op jit(solution)/shard_map/all_gather | solution.py:64
  102.7 15.3 %convolution_convert_fusion = bf16[512,4384]{0,1:T(8,128)(2,1)} fusion(bf16[2048,4384]{1,0:T(8,128)(2,1)} %all-gather.5.cloned.1.call-done, bf16[1,1,512,2048]{3,2,1,0:T(8,128)(2,1)S(1)} %copy-done), kind=kOutput, calls=%fused_computation.3 | convolution fusion | flops 9196158976 | bytes 24543232 | tf_op jit(solution)/shard_map/dot_general | solution.py:62
  118.0 1.8 slice.193
  119.9 0.9 fusion.61
  121.6 0.7 copy_bitcast_fusion.3
  123.3 0.7 fusion.60
  124.7 3.3 %collective-permute-start = (bf16[3,2304]{1,0:T(4,128)(2,1)S(1)}, bf16[3,2304]{1,0:T(4,128)(2,1)S(1)}, u32[]{:S(2)}, u32[]{:S(2)}) collective-permute-start(bf16[3,2304]{1,0:T(4,128)(2,1)S(1)} %copy.74), channel_id=1, source_target_pairs={{0,1},{1,2},{2,3},{4,5},{5,6},{6,7},{8,9},{9,10},{10,11},{12,13},{... | collective-permute-start | bytes 41480 | tf_op jit(solution)/shard_map/ppermute | solution.py:12
  128.5 1.2 reduce-window.26
  130.1 0.7 exponential_multiply_fusion
  132.0 10.5 %multiply_convert_fusion.2 = bf16[512,2304]{0,1:T(8,128)(2,1)S(1)} fusion(bf16[512,2304]{0,1:T(8,128)(2,1)} %copy-done.2, bf16[3,2304]{0,1:T(8,128)(2,1)S(1)} %copy.75, f32[2304]{0:T(1024)S(1)} %get-tuple-element.17, f32[2304]{0:T(1024)S(1)} %get-tuple-element.18, f32[2304]{0:T(1024)S(1)} %get-tuple-element.16, f32[2304]{0:T(1024)S(1)} %get-tuple-element.15, ...), kind=kLoop, calls=%fused_computation.6 | loop fusion | flops 30670848 | bytes 4778496 | tf_op jit(solution)/shard_map/convert_element_type | solution.py:78
  144.2 0.9 pad_maximum_fusion.1
  145.7 1.4 slice.227
  147.5 1.0 fusion.29
  148.5 1.0 fusion.36
  149.7 4.4 %bitcast_add_fusion.1 = f32[256,32,64]{0,2,1:T(8,128)} fusion(f32[256,32,64]{0,2,1:T(8,128)S(1)} %fusion.29, bf16[256,32,64]{0,2,1:T(8,128)(2,1)S(1)} %bitcast.347, f32[32,256]{1,0:T(8,128)S(1)} %copy-done.8, f32[32,256]{1,0:T(8,128)S(1)} %copy-done.4, f32[256,256]{1,0:T(8,128)S(1)} %fusion.45, pred[256,256]{1,0:T(8,128)(4,1)S(1)} %iota_compare_fusion, ...), kind=kOutput, calls=%fused_computation.44 | convolution fusion | flops 282066944 | bytes 5668864 | tf_op jit(solution)/shard_map/htu,uhp->thp/dot_general | solution.py:27
  154.2 4.3 %bitcast_add_fusion = f32[256,32,64]{0,2,1:T(8,128)} fusion(f32[256,32,64]{0,2,1:T(8,128)S(1)} %fusion.36, bf16[256,32,64]{0,2,1:T(8,128)(2,1)S(1)} %bitcast.346, f32[32,256]{1,0:T(8,128)S(1)} %copy-done.6, f32[32,256]{1,0:T(8,128)S(1)} %copy-done.5, f32[256,256]{1,0:T(8,128)S(1)} %fusion.40, pred[256,256]{1,0:T(8,128)(4,1)S(1)} %iota_compare_fusion, ...), kind=kOutput, calls=%fused_computation.43 | convolution fusion | flops 282066944 | bytes 5668864 | tf_op jit(solution)/shard_map/htu,uhp->thp/dot_general | solution.py:27
  158.5 17.3 %all-gather.7.cloned.1.call-done = bf16[128,8576]{1,0:T(8,128)(2,1)} async-done(((bf16[32,8576]{1,0:T(8,128)(2,1)}), bf16[128,8576]{1,0:T(8,128)(2,1)}) %all-gather.7.cloned.1.call-update) | async-done | bytes 2195472 | tf_op jit(solution)/shard_map/all_gather | solution.py:117
  175.8 2.0 slice_convert_fusion
  177.8 0.9 slice_convert_fusion.1
  178.7 1.6 slice_bitcast_fusion.2
  180.2 0.7 copy.110
  181.4 0.6 constant_dynamic-update-slice_fusion.31
  182.0 0.6 constant_dynamic-update-slice_fusion.30
  183.8 0.6 constant_dynamic-update-slice_fusion.27
  184.4 0.6 constant_dynamic-update-slice_fusion.26
  186.2 0.6 constant_dynamic-update-slice_fusion.23
  188.0 0.6 constant_dynamic-update-slice_fusion.20
  189.8 0.6 constant_dynamic-update-slice_fusion.17
  191.6 0.6 constant_dynamic-update-slice_fusion.14
  193.4 0.6 constant_dynamic-update-slice_fusion.11
  200.6 7.8 %all-to-all-start = ((f32[32,1,1,16,128]{4,3,2,1,0:T(8,128)}), f32[32,1,1,16,128]{4,3,2,1,0:T(8,128)}, u32[]{:S(2)}, u32[]{:S(2)}) async-start(f32[32,1,1,16,128]{4,3,2,1,0:T(8,128)} %constant_dynamic-update-slice_fusion), calls=%async_computation | async-start | bytes 524288 | tf_op jit(solution)/shard_map/all_to_all | solution.py:145
  208.4 1.4 copy.107
  209.8 1.4 copy.108
  211.6 0.8 fusion.26
  212.3 1.9 fusion.31
  214.3 3.7 %fusion.6 = f32[512,32,64]{0,2,1:T(8,128)S(1)} fusion(f32[256,32,64]{0,2,1:T(8,128)} %bitcast_add_fusion, f32[256,32,64]{0,2,1:T(8,128)} %bitcast_add_fusion.1, bf16[512,32,64]{0,2,1:T(8,128)(2,1)S(1)} %bitcast.305, f32[512,32,64]{0,2,1:T(8,128)S(1)} %fusion.31, f32[32]{0:T(128)S(1)} %copy-done.13, f32[512,32]{0,1:T(8,128)S(1)} %fusion.58), kind=kLoop, calls=%fused_computation.14 | loop fusion | flops 6291456 | bytes 14745728 | tf_op jit(solution)/shard_map/add | solution.py:131
  218.1 1.4 multiply_reduce_fusion
  219.5 2.9 %fusion.21 = bf16[1,1,512,2048]{2,3,1,0:T(8,128)(2,1)} fusion(f32[2048]{0:T(1024)S(1)} %copy-done.11, f32[512]{0:T(512)S(1)} %add_rsqrt_fusion, pred[512]{0:T(512)(128)(4,1)S(1)} %iota_compare_fusion.2, bf16[512,4384]{0,1:T(8,128)(2,1)S(1)} %bitcast.304, f32[512,32,64]{0,2,1:T(8,128)S(1)} %fusion.6), kind=kLoop, calls=%fused_computation.37 | loop fusion | flops 10485760 | bytes 8399360 | tf_op jit(solution)/shard_map/reshape | solution.py:138
  222.4 3.9 %copy.88 = bf16[1,1,512,2048]{3,2,1,0:T(8,128)(2,1)} copy(bf16[1,1,512,2048]{2,3,1,0:T(8,128)(2,1)} %fusion.21) | data formatting | bytes 4194304
  226.3 1.5 gather_fusion
  227.9 0.8 bitcast_select_fusion
  (115 shorter events, 22.6 us)
Async XLA Ops:
  7.2 95.5 %copy-start = (bf16[1,1,512,2048]{3,2,1,0:T(8,128)(2,1)S(1)}, bf16[1,1,512,2048]{3,2,1,0:T(8,128)(2,1)}, u32[]{:S(2)}) copy-start(bf16[1,1,512,2048]{3,2,1,0:T(8,128)(2,1)} %param.10) | copy-start | bytes 6291460
  7.2 95.5 %all-gather.5.cloned.1.call-start = ((), (), s32[]{:S(2)}) async-start(), calls=%async_computation.1 | async-start | bytes 18923520 | tf_op jit(solution)/shard_map/all_gather | solution.py:64
  21.8 154.0 %all-gather.7.cloned.1.call-start = ((), (), s32[]{:S(2)}) async-start(), calls=%async_computation.2 | async-start | bytes 2744320 | tf_op jit(solution)/shard_map/all_gather | solution.py:117
  118.0 1.9 copy-start.12
  118.0 14.0 %copy-start.10 = (f32[2304]{0:T(1024)S(1)}, f32[2304]{0:T(1024)}, u32[]{:S(2)}) copy-start(f32[2304]{0:T(1024)} %param.13) | copy-start | bytes 27652
  119.9 12.1 %copy-start.2 = (bf16[512,2304]{0,1:T(8,128)(2,1)}, bf16[512,2304]{0,1:T(8,128)(2,1)S(1)}, u32[]{:S(2)}) copy-start(bf16[512,2304]{0,1:T(8,128)(2,1)S(1)} %slice.193) | copy-start | bytes 7077892
  124.7 6.9 %collective-permute-start = (bf16[3,2304]{1,0:T(4,128)(2,1)S(1)}, bf16[3,2304]{1,0:T(4,128)(2,1)S(1)}, u32[]{:S(2)}, u32[]{:S(2)}) collective-permute-start(bf16[3,2304]{1,0:T(4,128)(2,1)S(1)} %copy.74), channel_id=1, source_target_pairs={{0,1},{1,2},{2,3},{4,5},{5,6},{6,7},{8,9},{9,10},{10,11},{12,13},{... | collective-permute-start | bytes 41480 | tf_op jit(solution)/shard_map/ppermute | solution.py:12
  132.0 10.9 %copy-start.14 = (f32[32]{0:T(128)S(1)}, f32[32]{0:T(128)}, u32[]{:S(2)}) copy-start(f32[32]{0:T(128)} %exponential_multiply_fusion.2) | copy-start | bytes 388
  142.5 0.9 copy-start.15
  148.5 1.2 copy-start.4
  148.5 1.2 copy-start.8
  148.5 1.2 copy-start.9
  149.7 4.5 %copy-start.5 = (f32[32,256]{1,0:T(8,128)S(1)}, f32[32,256]{1,0:T(8,128)}, u32[]{:S(2)}) copy-start(f32[32,256]{1,0:T(8,128)} %get-tuple-element.40) | copy-start | bytes 98308
  149.7 4.4 %copy-start.6 = (f32[32,256]{1,0:T(8,128)S(1)}, f32[32,256]{1,0:T(8,128)}, u32[]{:S(2)}) copy-start(f32[32,256]{1,0:T(8,128)} %get-tuple-element.32) | copy-start | bytes 98308
  149.7 4.4 %copy-start.7 = (f32[256,32]{0,1:T(8,128)S(1)}, f32[256,32]{0,1:T(8,128)}, u32[]{:S(2)}) copy-start(f32[256,32]{0,1:T(8,128)} %get-tuple-element.38) | copy-start | bytes 98308
  180.2 0.8 copy-start.16
  200.6 25.7 %all-to-all-start = ((f32[32,1,1,16,128]{4,3,2,1,0:T(8,128)}), f32[32,1,1,16,128]{4,3,2,1,0:T(8,128)}, u32[]{:S(2)}, u32[]{:S(2)}) async-start(f32[32,1,1,16,128]{4,3,2,1,0:T(8,128)} %constant_dynamic-update-slice_fusion), calls=%async_computation | async-start | bytes 524288 | tf_op jit(solution)/shard_map/all_to_all | solution.py:145
  211.6 2.7 %copy-start.3 = (bf16[512,2048]{0,1:T(8,128)(2,1)S(1)}, bf16[512,2048]{0,1:T(8,128)(2,1)}, u32[]{:S(2)}) copy-start(bf16[512,2048]{0,1:T(8,128)(2,1)} %slice.227) | copy-start | bytes 6291460
  211.6 2.7 %copy-start.13 = (f32[32]{0:T(128)S(1)}, f32[32]{0:T(128)}, u32[]{:S(2)}) copy-start(f32[32]{0:T(128)} %param.16) | copy-start | bytes 388
  212.3 5.7 %slice-start = ((s8[4489216]{0:T(1024)(128)(4,1)}), s8[4194304]{0:T(1024)(128)(4,1)S(1)}, s32[]{:S(2)}) async-start(s8[4489216]{0:T(1024)(128)(4,1)} %bitcast.303), calls=%async_computation.3 | async-start | bytes 8388608
  214.3 3.8 %slice-start.1 = ((s8[4489216]{0:T(1024)(128)(4,1)}), s8[294912]{0:T(1024)(128)(4,1)S(1)}, s32[]{:S(2)}) async-start(s8[4489216]{0:T(1024)(128)(4,1)} %bitcast.303), calls=%async_computation.4 | async-start | bytes 589824
  218.1 1.4 copy-start.11
  219.5 9.2 %copy-start.1 = (bf16[1,1,512,2048]{3,2,1,0:T(8,128)(2,1)S(1)}, bf16[1,1,512,2048]{3,2,1,0:T(8,128)(2,1)}, u32[]{:S(2)}) copy-start(bf16[1,1,512,2048]{3,2,1,0:T(8,128)(2,1)} %param.10) | copy-start | bytes 6291460
Sparse Core Ops, SparseCore 0:
  21.9 80.7 all-gather.4
  145.2 30.5 all-gather.6
